TPU v7x, 32 devices: a whole 2x2x4 slice. The times are simulated.
32 devices in a mesh: pool: 8 (over z, x), col: 4 (over y, core).
Axes of the slice: x: 2, y: 2, z: 4, core: 2. Of those that a mesh axis runs over, the one named last changes fastest.
Arguments:
- elements: float32 [8, 128, 2048], P('pool', None, 'col'), may hold values from -6 to 6
- index_map: int32 [8, 2048], P('pool', 'col'), may hold values from 0 to 2047, as said below
- band_energy: float32 [8], P('pool'), may hold values from 0.5 to 3
- eval_energy: float32 [2], replicated, may hold values from -1 to 1
- pole_strength: float32 [2048, 2048], P(None, 'col'), may hold values from -0.0078125 to 0.0078125
- pole_frequency: float32 [2048, 2048], P(None, 'col'), may hold values from 0.5 to 4
Outputs:
- sigma: float32 [2, 128, 128], replicated
Inputs may be any that keep to these rules, and one draw needn't show every extreme that they name: For every band, the entries of index_map in columns c * 512 to (c + 1) * 512 - 1 are those same indices in some order, for every column group c.
All inputs are finite; a program needn't handle non-finite values.
Results may differ from a plain program's by a relative error of at most 0.0003.
Values sent between devices are 32-bit elements; how exact they have to be, the bound alone decides.
No kernel may reach another device: no remote copies, remote signals or barrier semaphores. Data moves between devices by JAX's collectives and lax.ppermute only.
A program may use at most 64 MiB of HBM per device.

v0:
```python
import jax
import jax.numpy as jnp
from jax import lax
from jax.sharding import PartitionSpec as P

broadening = 0.5


def mix_rows(band_rows, pole_weight, pole_frequency, eval_energy, band_level):
    highest = lax.Precision.HIGHEST
    results = []
    for energy in range(eval_energy.shape[0]):
        offset = eval_energy[energy] - band_level - pole_frequency
        tile_now = pole_weight * offset / (offset * offset + broadening * broadening)
        results.append(
            jnp.dot(band_rows, tile_now, precision=highest, preferred_element_type=jnp.float32)
        )
    return jnp.concatenate(results, axis=1)


def permute_band(band_rows, band_index_row):
    highest = lax.Precision.HIGHEST
    columns = band_rows.shape[-1]
    source = lax.broadcasted_iota(jnp.int32, (columns, columns), 0)
    selector = (band_index_row[None, :] == source).astype(jnp.float32)
    return jnp.dot(band_rows, selector, precision=highest, preferred_element_type=jnp.float32)


def local(elements, index_map, band_energy, eval_energy, pole_strength, pole_frequency):
    highest = lax.Precision.HIGHEST
    states = elements.shape[1]
    columns = elements.shape[2]
    energies = eval_energy.shape[0]
    column_group = lax.axis_index("col")
    local_index = index_map - column_group * columns
    ordered = jnp.stack([permute_band(elements[0], local_index[0])])
    pole_weight = pole_strength / (2.0 * pole_frequency)
    mixed_list = mix_rows(
        lax.all_gather(ordered[0], "col", axis=1, tiled=True),
        pole_weight,
        pole_frequency,
        eval_energy,
        band_energy[0],
    )
    shaped = mixed_list.reshape(states, energies, columns)
    local_sigma = jnp.einsum("mej,nj->emn", shaped, ordered[0], precision=highest)
    result = lax.psum(local_sigma, ("pool", "col"))
    return result


def solution(mesh):
    placed = (
        P("pool", None, "col"),
        P("pool", "col"),
        P("pool"),
        P(),
        P(None, "col"),
        P(None, "col"),
    )
    return jax.shard_map(local, mesh=mesh, in_specs=placed, out_specs=P(), check_vma=False)
```

profile of v0, /device:TPU:0, one launch (start us, length us, event | category | flops | bytes accessed | tf_op | source)
XLA Modules:
  0.0 174.7 jit_solution(7117824040149415541)
XLA Ops:
  6.5 0.0 copy-start
  6.5 0.0 all-gather.2.cloned.1.call-start
  6.5 0.7 broadcast_subtract_fusion
  7.3 0.2 copy-done
  7.5 1.4 fusion.9
  8.9 0.0 all-gather.2.cloned.1.call-update
  8.9 0.0 all-reduce.2.cloned.1.call-start
  9.6 1.3 fusion.20
  12.2 16.3 %all-gather.2.cloned.1.call-done = f32[128,2048]{0,1:T(8,128)} async-done(((f32[128,512]{0,1:T(8,128)}), f32[128,2048]{0,1:T(8,128)}) %all-gather.2.cloned.1.call-update) | async-done | bytes 1048592 | tf_op jit(solution)/shard_map/all_gather | solution.py:39
  28.5 0.0 copy-start.2
  28.5 0.0 copy-start.3
  28.5 0.0 copy-start.4
  28.5 7.7 %fusion.1 = f32[128,512]{1,0:T(8,128)S(1)} fusion(f32[128,2048]{0,1:T(8,128)} %all-gather.2.cloned.1.call-done, f32[2048,512]{1,0:T(8,128)} %param.11, f32[2048,512]{1,0:T(8,128)} %param.10, f32[]{:T(128)} %bitcast.5), kind=kOutput, calls=%fused_computation.4 | convolution fusion | flops 1617952768 | bytes 9699332 | tf_op jit(solution)/shard_map/dot_general | solution.py:16
  36.2 0.0 copy-done.2
  36.3 0.0 copy-done.3
  36.3 0.0 copy-done.4
  36.3 0.0 copy-start.1
  36.3 3.9 %fusion = f32[128,512]{1,0:T(8,128)S(1)} fusion(f32[128,2048]{0,1:T(8,128)S(1)} %copy-done.4, f32[2048,512]{1,0:T(8,128)S(1)} %copy-done.2, f32[2048,512]{1,0:T(8,128)S(1)} %copy-done.3, f32[]{:T(128)} %bitcast.4), kind=kOutput, calls=%fused_computation.3 | convolution fusion | flops 1617952768 | bytes 9699332 | tf_op jit(solution)/shard_map/dot_general | solution.py:16
  40.3 0.0 copy-done.1
  40.3 1.3 convolution_bitcast_fusion
  41.5 0.0 all-reduce.2.cloned.1.call-update
  41.6 124.6 %all-reduce.2.cloned.1.call-done = f32[2,128,128]{1,2,0:T(8,128)} async-done(((f32[2,128,128]{1,2,0:T(8,128)}), f32[2,128,128]{1,2,0:T(8,128)}) %all-reduce.2.cloned.1.call-update) | async-done | bytes 131088 | tf_op jit(solution)/shard_map/psum | solution.py:47
  166.2 1.7 copy.9
  (1 shorter events, 0.0 us)
Async XLA Ops:
  6.5 1.0 copy-start
  6.5 22.0 %all-gather.2.cloned.1.call-start = ((), (), s32[]{:S(2)}) async-start(), calls=%async_computation | async-start | bytes 1310720 | tf_op jit(solution)/shard_map/all_gather | solution.py:39
  8.9 157.2 %all-reduce.2.cloned.1.call-start = ((), (), s32[]{:S(2)}) async-start(), calls=%async_computation.1 | async-start | bytes 262144 | tf_op jit(solution)/shard_map/psum | solution.py:47
  28.5 7.7 %copy-start.2 = (f32[2048,512]{1,0:T(8,128)S(1)}, f32[2048,512]{1,0:T(8,128)}, u32[]{:S(2)}) copy-start(f32[2048,512]{1,0:T(8,128)} %param.11) | copy-start | bytes 12582916
  28.5 7.7 %copy-start.3 = (f32[2048,512]{1,0:T(8,128)S(1)}, f32[2048,512]{1,0:T(8,128)}, u32[]{:S(2)}) copy-start(f32[2048,512]{1,0:T(8,128)} %param.10) | copy-start | bytes 12582916
  28.5 7.7 %copy-start.4 = (f32[128,2048]{0,1:T(8,128)S(1)}, f32[128,2048]{0,1:T(8,128)}, u32[]{:S(2)}) copy-start(f32[128,2048]{0,1:T(8,128)} %all-gather.2.cloned.1.call-done) | copy-start | bytes 3145732
  36.3 4.0 %copy-start.1 = (f32[512,128]{1,0:T(8,128)S(1)}, f32[512,128]{1,0:T(8,128)}, u32[]{:S(2)}) copy-start(f32[512,128]{1,0:T(8,128)} %fusion.9) | copy-start | bytes 786436
Sparse Core Ops, SparseCore 0:
  9.1 19.4 all-gather.1
  41.7 124.4 all-reduce.1
where the time goes:
time: 175 us
  waiting for transfers between devices  141 us (81%)
  between operations  15.4 us (9%)
  matrix products  14.3 us (8%)
  local copies, waits for them, and re-layouts  3.24 us (2%)
    psum x1, waiting for transfers between devices, local(): result = lax.psum(local_sigma, ('pool', 'col'))  125 us
    all_gather x1, waiting for transfers between devices, local(): lax.all_gather(ordered[0], 'col', axis=1, tiled=True)  16.3 us
    dot_general x2, matrix products, mix_rows(): jnp.dot(band_rows, tile_now, precision=highest, preferred_element_type=jn...  11.6 us
  transfers between devices with their start and end apart: 2, of which 2 were waited for; matrix products, arithmetic and copies ran while one was open for 1% of the time, Pallas kernels for 0%

commit v1 on v0

--- a/solution.py
+++ b/solution.py
@@ -4,6 +4,7 @@
 from jax.sharding import PartitionSpec as P
 
 broadening = 0.5
+test_the_slots = lambda local_x, mesh_dim: jnp.sum(lax.all_gather(local_x, mesh_dim), 0)
 
 
 def mix_rows(band_rows, pole_weight, pole_frequency, eval_energy, band_level):
@@ -44,7 +45,7 @@
     )
     shaped = mixed_list.reshape(states, energies, columns)
     local_sigma = jnp.einsum("mej,nj->emn", shaped, ordered[0], precision=highest)
-    result = lax.psum(local_sigma, ("pool", "col"))
+    result = test_the_slots(local_sigma, mesh_dim=("pool", "col"))
     return result
 
 

time: 175 us -> 114 us (0.65)
  waiting for transfers between devices: 141 us -> 78.1 us
  other arithmetic: 0.76 us -> 3.81 us
    psum x1 -> x0, waiting for transfers between devices: 125 us -> none  [local(): result = lax.psum(local_sigma, ('pool', 'col'))]
    all_gather x0 -> x1, waiting for transfers between devices: none -> 61.8 us  [lax.all_gather(local_x, mesh_dim)]
    reduce_sum x0 -> x1, other arithmetic: none -> 3.05 us  [jnp.sum(lax.all_gather(local_x, mesh_dim), 0)]
where the time goes in v1:
time: 114 us; the launch traced here: 113 us
  waiting for transfers between devices  78.1 us (69%)
  between operations  15.4 us (14%)
  matrix products  13.7 us (12%)
  other arithmetic  3.81 us (3%)
  local copies, waits for them, and re-layouts  2.34 us (2%)
    all_gather x1, waiting for transfers between devices, lax.all_gather(local_x, mesh_dim)  61.8 us
    all_gather x1, waiting for transfers between devices, local(): lax.all_gather(ordered[0], 'col', axis=1, tiled=True)  16.3 us
    dot_general x2, matrix products, mix_rows(): jnp.dot(band_rows, tile_now, precision=highest, preferred_element_type=jn...  11.6 us
    reduce_sum x1, other arithmetic, jnp.sum(lax.all_gather(local_x, mesh_dim), 0)  3.05 us
  transfers between devices with their start and end apart: 2, of which 2 were waited for; matrix products, arithmetic and copies ran while one was open for 1% of the time, Pallas kernels for 0%

profile of v1, /device:TPU:0, one launch (start us, length us, event | category | flops | bytes accessed | tf_op | source)
XLA Modules:
  0.0 113.3 jit_solution(5356710826908374951)
XLA Ops:
  6.5 0.0 copy-start
  6.5 0.0 all-gather.4.cloned.1.call-start
  6.5 0.7 broadcast_subtract_fusion
  7.3 0.2 copy-done
  7.5 1.4 %fusion.9 = f32[512,128]{1,0:T(8,128)} fusion(s32[512]{0:T(512)S(1)} %bitcast.22, f32[1,128,512]{2,1,0:T(8,128)S(1)} %copy-done), kind=kOutput, calls=%fused_computation.14 | convolution fusion | flops 403177472 | bytes 526336 | tf_op jit(solution)/shard_map/dot_general | solution.py:27
  8.9 0.0 all-gather.4.cloned.1.call-update
  8.9 0.0 all-gather.6.cloned.1.call-start
  9.6 1.3 %fusion.20 = (f32[1]{0:T(128)}, f32[1]{0:T(128)}) fusion(f32[2]{0:T(128)} %param.9), kind=kLoop, calls=%fused_computation.26 | loop fusion | bytes 16 | tf_op jit(solution)/shard_map/slice | solution.py:14
  12.2 16.3 %all-gather.4.cloned.1.call-done = f32[128,2048]{0,1:T(8,128)} async-done(((f32[128,512]{0,1:T(8,128)}), f32[128,2048]{0,1:T(8,128)}) %all-gather.4.cloned.1.call-update) | async-done | bytes 1048592 | tf_op jit(solution)/shard_map/all_gather | solution.py:40
  28.5 0.0 copy-start.2
  28.5 0.0 copy-start.3
  28.5 0.0 copy-start.4
  28.5 7.7 %fusion.1 = f32[128,512]{1,0:T(8,128)S(1)} fusion(f32[128,2048]{0,1:T(8,128)} %all-gather.4.cloned.1.call-done, f32[2048,512]{1,0:T(8,128)} %param.11, f32[2048,512]{1,0:T(8,128)} %param.10, f32[]{:T(128)} %bitcast.5), kind=kOutput, calls=%fused_computation.4 | convolution fusion | flops 1617952768 | bytes 9699332 | tf_op jit(solution)/shard_map/dot_general | solution.py:17
  36.2 0.0 copy-done.2
  36.3 0.0 copy-done.3
  36.3 0.0 copy-done.4
  36.3 0.0 copy-start.1
  36.3 3.9 %fusion = f32[128,512]{1,0:T(8,128)S(1)} fusion(f32[128,2048]{0,1:T(8,128)S(1)} %copy-done.4, f32[2048,512]{1,0:T(8,128)S(1)} %copy-done.2, f32[2048,512]{1,0:T(8,128)S(1)} %copy-done.3, f32[]{:T(128)} %bitcast.4), kind=kOutput, calls=%fused_computation.3 | convolution fusion | flops 1617952768 | bytes 9699332 | tf_op jit(solution)/shard_map/dot_general | solution.py:17
  40.3 0.0 copy-done.1
  40.3 0.6 convolution_bitcast_fusion
  40.9 0.8 copy.11
  41.6 0.0 all-gather.6.cloned.1.call-update
  41.7 61.8 %all-gather.6.cloned.1.call-done = f32[64,128,128]{2,1,0:T(8,128)} async-done(((f32[2,128,128]{2,1,0:T(8,128)}), f32[64,128,128]{2,1,0:T(8,128)}) %all-gather.6.cloned.1.call-update) | async-done | bytes 4194320 | tf_op jit(solution)/shard_map/all_gather | solution.py:7
  103.4 3.0 %reduce_sum.9 = f32[2,128,128]{2,1,0:T(8,128)} reduce(f32[32,2,128,128]{3,2,1,0:T(8,128)} %bitcast.19, f32[]{:T(128)} %constant.4.clone.1), dimensions={0}, to_apply=%region_0.0 | reduce | flops 1015808 | bytes 4325380 | tf_op jit(solution)/shard_map/reduce_sum | solution.py:7
  (1 shorter events, 0.0 us)
Async XLA Ops:
  6.5 1.0 copy-start
  6.5 22.0 %all-gather.4.cloned.1.call-start = ((), (), s32[]{:S(2)}) async-start(), calls=%async_computation | async-start | bytes 1310720 | tf_op jit(solution)/shard_map/all_gather | solution.py:40
  8.9 94.5 %all-gather.6.cloned.1.call-start = ((), (), s32[]{:S(2)}) async-start(), calls=%async_computation.1 | async-start | bytes 4325376 | tf_op jit(solution)/shard_map/all_gather | solution.py:7
  28.5 7.7 %copy-start.2 = (f32[2048,512]{1,0:T(8,128)S(1)}, f32[2048,512]{1,0:T(8,128)}, u32[]{:S(2)}) copy-start(f32[2048,512]{1,0:T(8,128)} %param.11) | copy-start | bytes 12582916
  28.5 7.7 %copy-start.3 = (f32[2048,512]{1,0:T(8,128)S(1)}, f32[2048,512]{1,0:T(8,128)}, u32[]{:S(2)}) copy-start(f32[2048,512]{1,0:T(8,128)} %param.10) | copy-start | bytes 12582916
  28.5 7.7 %copy-start.4 = (f32[128,2048]{0,1:T(8,128)S(1)}, f32[128,2048]{0,1:T(8,128)}, u32[]{:S(2)}) copy-start(f32[128,2048]{0,1:T(8,128)} %all-gather.4.cloned.1.call-done) | copy-start | bytes 3145732
  36.3 4.0 %copy-start.1 = (f32[512,128]{1,0:T(8,128)S(1)}, f32[512,128]{1,0:T(8,128)}, u32[]{:S(2)}) copy-start(f32[512,128]{1,0:T(8,128)} %fusion.9) | copy-start | bytes 786436
Sparse Core Ops, SparseCore 0:
  9.1 19.4 all-gather.3
  41.8 61.6 all-gather.5
